TPU v7x, 512 devices: a whole 4x8x8 slice. The times are simulated.
512 devices in a mesh: seq: 64 (over z_hi, y, core), ch: 8 (over x, z_lo).
Axes of the slice: x: 4, y: 8, z: 8 (z_hi: 4, z_lo: 2; z = z_hi * 2 + z_lo), core: 2. Of those that a mesh axis runs over, the one named last changes fastest.
Arguments:
- inputs: bfloat16 [262144, 2048], P('seq', 'ch'), may hold values from -6 to 6
- first_factor: bfloat16 [512, 512], P('ch'), may hold values from -0.25 to 0.25
- twiddle: float32 [512, 512], P('seq'), may hold values from -4 to 4
- second_factor: bfloat16 [512, 512], P('ch'), may hold values from -0.25 to 0.25
- block_first: bfloat16 [64, 32, 32], P('ch'), may hold values from -1 to 1
- block_second: bfloat16 [32, 64, 64], P('ch'), may hold values from -0.75 to 0.75
Outputs:
- mixed_out: bfloat16 [262144, 2048], P('seq', 'ch')
All inputs are finite; a program needn't handle non-finite values.
Results may differ from a plain program's by a relative error of at most 0.007.
Values may be sent and summed in bfloat16 or wider, within the bound.
No kernel may reach another device: no remote copies, remote signals or barrier semaphores. Data moves between devices by JAX's collectives and lax.ppermute only.
A program may use at most 128 MiB of HBM per device.

v0:
```python
import jax
import jax.numpy as jnp
from jax import lax
from jax.sharding import PartitionSpec as P

BLOCK = 512
CHUNKS = 2


def channel_weights(block_first, block_second, n_ch):
    n_a, n_m, n_b = block_first.shape
    m_l = n_m // n_ch
    bf = jnp.transpose(block_first, (1, 0, 2))
    bf = bf.reshape(n_ch, m_l, n_a, 1, n_b)
    eye_a = jnp.eye(n_a, dtype=jnp.bool_).reshape(1, 1, n_a, n_a, 1)
    w1t = jnp.where(eye_a, bf, jnp.zeros((), bf.dtype))
    w1t = w1t.reshape(n_ch * m_l * n_a, n_a * n_b)
    n_m2, n_p, n_a2 = block_second.shape
    a_l = n_a2 // n_ch
    bs = block_second.reshape(n_m2, n_p, n_ch, a_l)
    bs = jnp.transpose(bs, (2, 0, 3, 1))
    bs = bs.reshape(n_ch, n_m2, a_l, 1, n_p)
    eye_m = jnp.eye(n_m2, dtype=jnp.bool_).reshape(1, n_m2, 1, n_m2, 1)
    w2 = jnp.where(eye_m, bs, jnp.zeros((), bs.dtype))
    w2 = w2.reshape(n_ch * n_m2 * a_l, n_m2 * n_p)
    return (w1t, w2)


def make_local(n_seq, n_ch):

    def local(inputs, first_factor, twiddle, second_factor, block_first, block_second):
        tok_rows, channels = inputs.shape
        outer_rows = tok_rows // BLOCK
        token_grid = inputs.reshape(outer_rows, BLOCK, channels)
        rows = first_factor.shape[0]
        both = lax.all_gather(
            jnp.concatenate([first_factor, second_factor], axis=0), "ch", axis=0, tiled=True
        ).reshape(n_ch, 2, rows, BLOCK)
        full_first = both[:, 0].reshape(BLOCK, BLOCK)
        full_second = both[:, 1].reshape(BLOCK, BLOCK)
        twiddle_t = jnp.transpose(twiddle)
        w1t, w2 = channel_weights(block_first, block_second, n_ch)
        contract = (((1,), (1,)), ((), ()))
        width = BLOCK // CHUNKS
        outs = []
        for q in range(CHUNKS):
            lo = q * width
            first = lax.dot_general(
                full_first[lo : lo + width],
                token_grid,
                contract,
                preferred_element_type=jnp.float32,
            )
            twisted = (first * twiddle_t[lo : lo + width, :, None]).astype(jnp.bfloat16)
            gathered = lax.all_to_all(twisted, "seq", split_axis=0, concat_axis=1, tiled=True)
            mixed = lax.dot_general(
                full_second, gathered, contract, preferred_element_type=jnp.float32
            ).astype(jnp.bfloat16)
            returned = lax.all_to_all(mixed, "seq", split_axis=0, concat_axis=1, tiled=True)
            gated = (
                token_grid[:, lo : lo + width].astype(jnp.float32) * returned.astype(jnp.float32)
            ).astype(jnp.bfloat16)
            gated = gated.reshape(outer_rows * width, channels)
            middle_t = lax.dot_general(
                w1t, gated, contract, preferred_element_type=jnp.float32
            ).astype(jnp.bfloat16)
            middle_t = middle_t.reshape(n_ch, channels // n_ch, outer_rows * width)
            recv = lax.all_to_all(middle_t, "ch", split_axis=0, concat_axis=0, tiled=True)
            recv = recv.reshape(channels, outer_rows * width)
            result = lax.dot_general(
                recv, w2, (((0,), (0,)), ((), ())), preferred_element_type=jnp.float32
            ).astype(jnp.bfloat16)
            outs.append(result.reshape(outer_rows, width, channels))
        out = jnp.concatenate(outs, axis=1)
        return out.reshape(tok_rows, channels)

    return local


def solution(mesh):
    placed = (
        P("seq", "ch"),
        P("ch", None),
        P("seq", None),
        P("ch", None),
        P("ch", None, None),
        P("ch", None, None),
    )
    return jax.shard_map(
        make_local(mesh.shape["seq"], mesh.shape["ch"]),
        mesh=mesh,
        in_specs=placed,
        out_specs=P("seq", "ch"),
        check_vma=False,
    )
```

profile of v0, /device:TPU:24, one launch (start us, length us, event | category | flops | bytes accessed | tf_op | source)
XLA Modules:
  0.0 274.9 jit_solution(7449750613190882592)
XLA Ops:
  6.5 0.0 all-gather.2.cloned.1.call-start
  6.5 1.5 pad_maximum_fusion.1
  8.1 0.0 all-gather.2.cloned.1.call-update
  8.1 0.7 fusion.5
  8.8 51.1 %all-gather.2.cloned.1.call-done = bf16[1024,512]{1,0:T(8,128)(2,1)} async-done(((bf16[128,512]{1,0:T(8,128)(2,1)}), bf16[1024,512]{1,0:T(8,128)(2,1)}) %all-gather.2.cloned.1.call-update) | async-done | bytes 1048592 | tf_op jit(solution)/shard_map/all_gather | solution.py:36
  59.9 1.1 fusion.4
  61.0 2.3 multiply_convert_fusion.3
  63.3 0.0 copy-start
  63.3 1.6 copy.29
  64.9 12.4 %all-to-all-start = ((bf16[256,8,256]{2,1,0:T(8,128)(2,1)}), bf16[256,8,256]{2,1,0:T(8,128)(2,1)S(1)}, u32[]{:S(2)}, u32[]{:S(2)}) async-start(bf16[256,8,256]{2,1,0:T(8,128)(2,1)} %copy.29), calls=%async_computation | async-start | bytes 2097152 | tf_op jit(solution)/shard_map/all_to_all | solution.py:55
  77.3 0.0 copy-done
  77.3 0.7 multiply_convert_fusion.1
  78.0 1.6 copy.36
  79.6 25.8 %all-to-all-done = bf16[256,8,256]{2,1,0:T(8,128)(2,1)S(1)} async-done(((bf16[256,8,256]{2,1,0:T(8,128)(2,1)}), bf16[256,8,256]{2,1,0:T(8,128)(2,1)S(1)}, u32[]{:S(2)}, u32[]{:S(2)}) %all-to-all-start) | async-done | bytes 1048608 | tf_op jit(solution)/shard_map/all_to_all | solution.py:55
  105.4 8.5 %all-to-all-start.3 = ((bf16[256,8,256]{2,1,0:T(8,128)(2,1)}), bf16[256,8,256]{2,1,0:T(8,128)(2,1)S(1)}, u32[]{:S(2)}, u32[]{:S(2)}) async-start(bf16[256,8,256]{2,1,0:T(8,128)(2,1)} %copy.36), calls=%async_computation.3 | async-start | bytes 2097152 | tf_op jit(solution)/shard_map/all_to_all | solution.py:55
  113.9 0.8 copy-done.2
  114.7 0.7 convolution_convert_fusion.5
  115.5 1.8 copy.31
  117.2 25.0 %all-to-all-done.3 = bf16[256,8,256]{2,1,0:T(8,128)(2,1)S(1)} async-done(((bf16[256,8,256]{2,1,0:T(8,128)(2,1)}), bf16[256,8,256]{2,1,0:T(8,128)(2,1)S(1)}, u32[]{:S(2)}, u32[]{:S(2)}) %all-to-all-start.3) | async-done | bytes 1048608 | tf_op jit(solution)/shard_map/all_to_all | solution.py:55
  142.2 9.0 %all-to-all-start.1 = ((bf16[512,4,256]{2,1,0:T(4,128)(2,1)}), bf16[512,4,256]{2,1,0:T(4,128)(2,1)S(1)}, u32[]{:S(2)}, u32[]{:S(2)}) async-start(bf16[512,4,256]{2,1,0:T(4,128)(2,1)} %copy.31), calls=%async_computation.1 | async-start | bytes 2097152 | tf_op jit(solution)/shard_map/all_to_all | solution.py:59
  151.2 0.7 convolution_convert_fusion.4
  151.9 0.0 copy-start.4
  151.9 1.8 copy.38
  153.8 25.7 %all-to-all-done.1 = bf16[512,4,256]{2,1,0:T(4,128)(2,1)S(1)} async-done(((bf16[512,4,256]{2,1,0:T(4,128)(2,1)}), bf16[512,4,256]{2,1,0:T(4,128)(2,1)S(1)}, u32[]{:S(2)}, u32[]{:S(2)}) %all-to-all-start.1) | async-done | bytes 1048608 | tf_op jit(solution)/shard_map/all_to_all | solution.py:59
  179.5 9.3 %all-to-all-start.4 = ((bf16[512,4,256]{2,1,0:T(4,128)(2,1)}), bf16[512,4,256]{2,1,0:T(4,128)(2,1)S(1)}, u32[]{:S(2)}, u32[]{:S(2)}) async-start(bf16[512,4,256]{2,1,0:T(4,128)(2,1)} %copy.38), calls=%async_computation.4 | async-start | bytes 2097152 | tf_op jit(solution)/shard_map/all_to_all | solution.py:59
  188.8 0.1 broadcast_select_fusion
  188.9 0.4 select_n.37
  189.3 0.3 convert_bitcast_fusion.1
  189.6 0.4 copy.32
  190.0 1.7 reshape.114
  191.7 25.3 %all-to-all-done.4 = bf16[512,4,256]{2,1,0:T(4,128)(2,1)S(1)} async-done(((bf16[512,4,256]{2,1,0:T(4,128)(2,1)}), bf16[512,4,256]{2,1,0:T(4,128)(2,1)S(1)}, u32[]{:S(2)}, u32[]{:S(2)}) %all-to-all-start.4) | async-done | bytes 1048608 | tf_op jit(solution)/shard_map/all_to_all | solution.py:59
  217.0 0.3 convert_bitcast_fusion
  217.3 0.4 copy.39
  217.7 1.7 reshape.115
  219.4 3.4 %multiply_convert_fusion.2 = (bf16[8,256,256]{2,1,0:T(8,128)(2,1)S(1)}, bf16[8,256,256]{2,1,0:T(8,128)(2,1)S(1)}) fusion(f32[8,256,256]{2,1,0:T(8,128)} %reshape.114, bf16[8,512,256]{2,1,0:T(8,128)(2,1)} %bitcast.81, f32[8,256,256]{2,1,0:T(8,128)} %reshape.115), kind=kLoop, calls=%fused_computation.9 | loop fusion | flops 3145728 | bytes 8388608 | tf_op jit(solution)/shard_map/convert_element_type | solution.py:62
  222.8 1.5 convolution_convert_fusion.3
  224.3 5.2 %all-to-all-start.2 = ((bf16[8,32,2048]{2,1,0:T(8,128)(2,1)}), bf16[8,32,2048]{2,1,0:T(8,128)(2,1)S(1)}, u32[]{:S(2)}, u32[]{:S(2)}) async-start(bf16[8,32,2048]{2,1,0:T(8,128)(2,1)} %bitcast.15), calls=%async_computation.2 | async-start | bytes 2097152 | tf_op jit(solution)/shard_map/all_to_all | solution.py:68
  229.5 1.4 convolution_convert_fusion.1
  230.9 15.0 %all-to-all-done.2 = bf16[8,32,2048]{2,1,0:T(8,128)(2,1)S(1)} async-done(((bf16[8,32,2048]{2,1,0:T(8,128)(2,1)}), bf16[8,32,2048]{2,1,0:T(8,128)(2,1)S(1)}, u32[]{:S(2)}, u32[]{:S(2)}) %all-to-all-start.2) | async-done | bytes 1048608 | tf_op jit(solution)/shard_map/all_to_all | solution.py:68
  245.9 3.6 %all-to-all-start.5 = ((bf16[8,32,2048]{2,1,0:T(8,128)(2,1)}), bf16[8,32,2048]{2,1,0:T(8,128)(2,1)S(1)}, u32[]{:S(2)}, u32[]{:S(2)}) async-start(bf16[8,32,2048]{2,1,0:T(8,128)(2,1)} %bitcast.29), calls=%async_computation.5 | async-start | bytes 2097152 | tf_op jit(solution)/shard_map/all_to_all | solution.py:68
  249.5 0.0 copy-done.5
  249.5 0.1 copy.33
  249.6 0.2 broadcast_select_fusion.1
  249.8 0.2 select_n.39
  250.0 0.5 convolution_convert_fusion.2
  250.5 15.6 %all-to-all-done.5 = bf16[8,32,2048]{2,1,0:T(8,128)(2,1)S(1)} async-done(((bf16[8,32,2048]{2,1,0:T(8,128)(2,1)}), bf16[8,32,2048]{2,1,0:T(8,128)(2,1)S(1)}, u32[]{:S(2)}, u32[]{:S(2)}) %all-to-all-start.5) | async-done | bytes 1048608 | tf_op jit(solution)/shard_map/all_to_all | solution.py:68
  266.1 0.5 convolution_convert_fusion
  266.6 1.5 pad_maximum_fusion
  (11 shorter events, 0.1 us)
Async XLA Ops:
  6.5 53.4 %all-gather.2.cloned.1.call-start = ((), (), s32[]{:S(2)}) async-start(), calls=%async_computation.6 | async-start | bytes 1179648 | tf_op jit(solution)/shard_map/all_gather | solution.py:36
  63.3 14.0 %copy-start = (bf16[4096,256]{1,0:T(8,128)(2,1)S(1)}, bf16[4096,256]{1,0:T(8,128)(2,1)}, u32[]{:S(2)}) copy-start(bf16[4096,256]{1,0:T(8,128)(2,1)} %param.6) | copy-start | bytes 6291460
  64.9 40.5 %all-to-all-start = ((bf16[256,8,256]{2,1,0:T(8,128)(2,1)}), bf16[256,8,256]{2,1,0:T(8,128)(2,1)S(1)}, u32[]{:S(2)}, u32[]{:S(2)}) async-start(bf16[256,8,256]{2,1,0:T(8,128)(2,1)} %copy.29), calls=%async_computation | async-start | bytes 2097152 | tf_op jit(solution)/shard_map/all_to_all | solution.py:55
  78.0 35.8 %copy-start.1 = (bf16[1024,512]{1,0:T(8,128)(2,1)S(1)}, bf16[1024,512]{1,0:T(8,128)(2,1)}, u32[]{:S(2)}) copy-start(bf16[1024,512]{1,0:T(8,128)(2,1)} %all-gather.2.cloned.1.call-done) | copy-start | bytes 3145732
  105.4 36.8 %all-to-all-start.3 = ((bf16[256,8,256]{2,1,0:T(8,128)(2,1)}), bf16[256,8,256]{2,1,0:T(8,128)(2,1)S(1)}, u32[]{:S(2)}, u32[]{:S(2)}) async-start(bf16[256,8,256]{2,1,0:T(8,128)(2,1)} %copy.36), calls=%async_computation.3 | async-start | bytes 2097152 | tf_op jit(solution)/shard_map/all_to_all | solution.py:55
  113.9 0.8 copy-start.2
  115.4 35.8 %copy-start.3 = (bf16[8,1,64,512]{3,2,1,0:T(8,128)(2,1)S(1)}, bf16[8,1,64,512]{3,2,1,0:T(8,128)(2,1)}, u32[]{:S(2)}) copy-start(bf16[8,1,64,512]{3,2,1,0:T(8,128)(2,1)} %copy-done.2) | copy-start | bytes 1572868
  142.2 37.2 %all-to-all-start.1 = ((bf16[512,4,256]{2,1,0:T(4,128)(2,1)}), bf16[512,4,256]{2,1,0:T(4,128)(2,1)S(1)}, u32[]{:S(2)}, u32[]{:S(2)}) async-start(bf16[512,4,256]{2,1,0:T(4,128)(2,1)} %copy.31), calls=%async_computation.1 | async-start | bytes 2097152 | tf_op jit(solution)/shard_map/all_to_all | solution.py:59
  151.9 36.8 %copy-start.4 = (bf16[8,32,32]{2,1,0:T(8,128)(2,1)S(1)}, bf16[8,32,32]{2,1,0:T(8,128)(2,1)}, u32[]{:S(2)}) copy-start(bf16[8,32,32]{2,1,0:T(8,128)(2,1)} %param.10) | copy-start | bytes 49156
  179.5 37.5 %all-to-all-start.4 = ((bf16[512,4,256]{2,1,0:T(4,128)(2,1)}), bf16[512,4,256]{2,1,0:T(4,128)(2,1)S(1)}, u32[]{:S(2)}, u32[]{:S(2)}) async-start(bf16[512,4,256]{2,1,0:T(4,128)(2,1)} %copy.38), calls=%async_computation.4 | async-start | bytes 2097152 | tf_op jit(solution)/shard_map/all_to_all | solution.py:59
  224.3 21.6 %all-to-all-start.2 = ((bf16[8,32,2048]{2,1,0:T(8,128)(2,1)}), bf16[8,32,2048]{2,1,0:T(8,128)(2,1)S(1)}, u32[]{:S(2)}, u32[]{:S(2)}) async-start(bf16[8,32,2048]{2,1,0:T(8,128)(2,1)} %bitcast.15), calls=%async_computation.2 | async-start | bytes 2097152 | tf_op jit(solution)/shard_map/all_to_all | solution.py:68
  229.5 20.0 %copy-start.5 = (bf16[4,64,64]{2,1,0:T(8,128)(2,1)S(1)}, bf16[4,64,64]{2,1,0:T(8,128)(2,1)}, u32[]{:S(2)}) copy-start(bf16[4,64,64]{2,1,0:T(8,128)(2,1)} %param.11) | copy-start | bytes 98308
  245.9 20.2 %all-to-all-start.5 = ((bf16[8,32,2048]{2,1,0:T(8,128)(2,1)}), bf16[8,32,2048]{2,1,0:T(8,128)(2,1)S(1)}, u32[]{:S(2)}, u32[]{:S(2)}) async-start(bf16[8,32,2048]{2,1,0:T(8,128)(2,1)} %bitcast.29), calls=%async_computation.5 | async-start | bytes 2097152 | tf_op jit(solution)/shard_map/all_to_all | solution.py:68
Sparse Core Ops, SparseCore 0:
  9.4 50.4 all-gather.1
where the time goes:
time: 276 us; the launch traced here: 275 us
  waiting for transfers between devices  183 us (66%)
  starting transfers between devices  47.9 us (17%)
  local copies, waits for them, and re-layouts  14.3 us (5%)
  between operations  13.7 us (5%)
  matrix products  8.32 us (3%)
  other arithmetic  7.35 us (3%)
    all_gather x1, waiting for transfers between devices, local(): lax.all_gather(jnp.concatenate([first_factor, second_factor], axis=0), 'c...  51.1 us
    all_to_all x2, waiting for transfers between devices, local(): lax.all_to_all(mixed, 'seq', split_axis=0, concat_axis=1, tiled=True)  51 us
    all_to_all x2, waiting for transfers between devices, local(): lax.all_to_all(twisted, 'seq', split_axis=0, concat_axis=1, tiled=True)  50.8 us
    all_to_all x2, waiting for transfers between devices, local(): lax.all_to_all(middle_t, 'ch', split_axis=0, concat_axis=0, tiled=True)  30.6 us
    all_to_all x2, starting transfers between devices, local(): lax.all_to_all(twisted, 'seq', split_axis=0, concat_axis=1, tiled=True)  20.9 us
    all_to_all x2, starting transfers between devices, local(): lax.all_to_all(mixed, 'seq', split_axis=0, concat_axis=1, tiled=True)  18.2 us
    all_to_all x2, starting transfers between devices, local(): lax.all_to_all(middle_t, 'ch', split_axis=0, concat_axis=0, tiled=True)  8.74 us
  transfers between devices with their start and end apart: 7, of which 7 were waited for; matrix products, arithmetic and copies ran while one was open for 5% of the time, Pallas kernels for 0%

commit v1 on v0

--- a/solution.py
+++ b/solution.py
@@ -33,8 +33,16 @@
         outer_rows = tok_rows // BLOCK
         token_grid = inputs.reshape(outer_rows, BLOCK, channels)
         rows = first_factor.shape[0]
-        both = lax.all_gather(
-            jnp.concatenate([first_factor, second_factor], axis=0), "ch", axis=0, tiled=True
+        both = jnp.concatenate(
+            lax.all_to_all(
+                jnp.stack(
+                    [jnp.concatenate([first_factor, second_factor], axis=0)] * lax.axis_size("ch")
+                ),
+                "ch",
+                0,
+                0,
+            ),
+            axis=0,
         ).reshape(n_ch, 2, rows, BLOCK)
         full_first = both[:, 0].reshape(BLOCK, BLOCK)
         full_second = both[:, 1].reshape(BLOCK, BLOCK)

time: 276 us -> 233 us (0.84)
  waiting for transfers between devices: 183 us -> 148 us
  between operations: 13.7 us -> 0.26 us
  starting transfers between devices: 47.9 us -> 57.3 us
    all_gather x1 -> x0, waiting for transfers between devices: 51.1 us -> none  [local(): lax.all_gather(jnp.concatenate([first_factor, second_factor], axis=0), 'c...]
    all_to_all x0 -> x1, waiting for transfers between devices: none -> 15.7 us  [local(): lax.all_to_all(jnp.stack([jnp.concatenate([first_factor, second_factor],...]
    all_to_all x0 -> x1, starting transfers between devices: none -> 6.11 us  [local(): lax.all_to_all(jnp.stack([jnp.concatenate([first_factor, second_factor],...]
    all_to_all x2, starting transfers between devices: 20.9 us -> 25.1 us  [local(): lax.all_to_all(twisted, 'seq', split_axis=0, concat_axis=1, tiled=True)]
  transfers between devices with their start and end apart: 7 -> 7, of which waited for: 7 -> 7; matrix products, arithmetic and copies ran while one was open for 5% -> 6% of each run, Pallas kernels for 0% -> 0%
where the time goes in v1:
time: 233 us
  waiting for transfers between devices  148 us (64%)
  starting transfers between devices  57.3 us (25%)
  local copies, waits for them, and re-layouts  12.8 us (5%)
  matrix products  7.94 us (3%)
  other arithmetic  6.71 us (3%)
    all_to_all x2, waiting for transfers between devices, local(): lax.all_to_all(mixed, 'seq', split_axis=0, concat_axis=1, tiled=True)  51.2 us
    all_to_all x2, waiting for transfers between devices, local(): lax.all_to_all(twisted, 'seq', split_axis=0, concat_axis=1, tiled=True)  50.4 us
    all_to_all x2, waiting for transfers between devices, local(): lax.all_to_all(middle_t, 'ch', split_axis=0, concat_axis=0, tiled=True)  30.5 us
    all_to_all x2, starting transfers between devices, local(): lax.all_to_all(twisted, 'seq', split_axis=0, concat_axis=1, tiled=True)  25.1 us
    all_to_all x2, starting transfers between devices, local(): lax.all_to_all(mixed, 'seq', split_axis=0, concat_axis=1, tiled=True)  19 us
    all_to_all x1, waiting for transfers between devices, local(): lax.all_to_all(jnp.stack([jnp.concatenate([first_factor, second_factor],...  15.7 us
    all_to_all x2, starting transfers between devices, local(): lax.all_to_all(middle_t, 'ch', split_axis=0, concat_axis=0, tiled=True)  7.12 us
    all_to_all x1, starting transfers between devices, local(): lax.all_to_all(jnp.stack([jnp.concatenate([first_factor, second_factor],...  6.11 us
  transfers between devices with their start and end apart: 7, of which 7 were waited for; matrix products, arithmetic and copies ran while one was open for 6% of the time, Pallas kernels for 0%

profile of v1, /device:TPU:24, one launch (start us, length us, event | category | flops | bytes accessed | tf_op | source)
XLA Modules:
  0.0 232.8 jit_solution(8422021919565129018)
XLA Ops:
  0.0 0.9 pad_maximum_fusion.1
  0.9 0.0 copy-start
  0.9 1.1 stack.2
  2.0 6.1 %all-to-all-start = ((bf16[8,128,512]{2,1,0:T(8,128)(2,1)}), bf16[8,128,512]{2,1,0:T(8,128)(2,1)S(1)}, u32[]{:S(2)}, u32[]{:S(2)}) async-start(bf16[8,128,512]{2,1,0:T(8,128)(2,1)} %stack.2), calls=%async_computation | async-start | bytes 2097152 | tf_op jit(solution)/shard_map/all_to_all | solution.py:37
  8.1 0.0 copy-done.3
  8.1 15.7 %all-to-all-done = bf16[8,128,512]{2,1,0:T(8,128)(2,1)S(1)} async-done(((bf16[8,128,512]{2,1,0:T(8,128)(2,1)}), bf16[8,128,512]{2,1,0:T(8,128)(2,1)S(1)}, u32[]{:S(2)}, u32[]{:S(2)}) %all-to-all-start) | async-done | bytes 1048608 | tf_op jit(solution)/shard_map/all_to_all | solution.py:37
  23.8 0.0 copy-done
  23.8 0.7 multiply_convert_fusion.1
  24.6 1.6 copy.27
  26.1 15.6 %all-to-all-start.4 = ((bf16[256,8,256]{2,1,0:T(8,128)(2,1)}), bf16[256,8,256]{2,1,0:T(8,128)(2,1)}, u32[]{:S(2)}, u32[]{:S(2)}) async-start(bf16[256,8,256]{2,1,0:T(8,128)(2,1)} %copy.27), calls=%async_computation.4 | async-start | bytes 2097152 | tf_op jit(solution)/shard_map/all_to_all | solution.py:63
  41.8 0.7 multiply_convert_fusion.3
  42.5 1.6 copy.21
  44.0 25.9 %all-to-all-done.4 = bf16[256,8,256]{2,1,0:T(8,128)(2,1)} async-done(((bf16[256,8,256]{2,1,0:T(8,128)(2,1)}), bf16[256,8,256]{2,1,0:T(8,128)(2,1)}, u32[]{:S(2)}, u32[]{:S(2)}) %all-to-all-start.4) | async-done | bytes 1048608 | tf_op jit(solution)/shard_map/all_to_all | solution.py:63
  70.0 9.5 %all-to-all-start.1 = ((bf16[256,8,256]{2,1,0:T(8,128)(2,1)}), bf16[256,8,256]{2,1,0:T(8,128)(2,1)S(1)}, u32[]{:S(2)}, u32[]{:S(2)}) async-start(bf16[256,8,256]{2,1,0:T(8,128)(2,1)} %copy.21), calls=%async_computation.1 | async-start | bytes 2097152 | tf_op jit(solution)/shard_map/all_to_all | solution.py:63
  79.5 1.9 convolution_convert_fusion.4
  81.4 1.8 copy.29
  83.2 24.5 %all-to-all-done.1 = bf16[256,8,256]{2,1,0:T(8,128)(2,1)S(1)} async-done(((bf16[256,8,256]{2,1,0:T(8,128)(2,1)}), bf16[256,8,256]{2,1,0:T(8,128)(2,1)S(1)}, u32[]{:S(2)}, u32[]{:S(2)}) %all-to-all-start.1) | async-done | bytes 1048608 | tf_op jit(solution)/shard_map/all_to_all | solution.py:63
  107.7 9.5 %all-to-all-start.5 = ((bf16[512,4,256]{2,1,0:T(4,128)(2,1)}), bf16[512,4,256]{2,1,0:T(4,128)(2,1)S(1)}, u32[]{:S(2)}, u32[]{:S(2)}) async-start(bf16[512,4,256]{2,1,0:T(4,128)(2,1)} %copy.29), calls=%async_computation.5 | async-start | bytes 2097152 | tf_op jit(solution)/shard_map/all_to_all | solution.py:67
  117.2 0.7 convolution_convert_fusion.5
  117.9 0.0 copy-start.1
  117.9 1.8 copy.23
  119.7 25.8 %all-to-all-done.5 = bf16[512,4,256]{2,1,0:T(4,128)(2,1)S(1)} async-done(((bf16[512,4,256]{2,1,0:T(4,128)(2,1)}), bf16[512,4,256]{2,1,0:T(4,128)(2,1)S(1)}, u32[]{:S(2)}, u32[]{:S(2)}) %all-to-all-start.5) | async-done | bytes 1048608 | tf_op jit(solution)/shard_map/all_to_all | solution.py:67
  145.5 9.5 %all-to-all-start.2 = ((bf16[512,4,256]{2,1,0:T(4,128)(2,1)}), bf16[512,4,256]{2,1,0:T(4,128)(2,1)S(1)}, u32[]{:S(2)}, u32[]{:S(2)}) async-start(bf16[512,4,256]{2,1,0:T(4,128)(2,1)} %copy.23), calls=%async_computation.2 | async-start | bytes 2097152 | tf_op jit(solution)/shard_map/all_to_all | solution.py:67
  155.0 0.0 copy-done.1
  155.0 0.1 broadcast_select_fusion
  155.2 0.4 select_n.37
  155.5 0.3 convert_bitcast_fusion
  155.8 0.4 copy.30
  156.2 1.7 reshape.113
  158.0 25.4 %all-to-all-done.2 = bf16[512,4,256]{2,1,0:T(4,128)(2,1)S(1)} async-done(((bf16[512,4,256]{2,1,0:T(4,128)(2,1)}), bf16[512,4,256]{2,1,0:T(4,128)(2,1)S(1)}, u32[]{:S(2)}, u32[]{:S(2)}) %all-to-all-start.2) | async-done | bytes 1048608 | tf_op jit(solution)/shard_map/all_to_all | solution.py:67
  183.3 0.3 convert_bitcast_fusion.1
  183.7 0.4 copy.24
  184.0 1.7 reshape.112
  185.8 3.4 %multiply_convert_fusion.2 = (bf16[8,256,256]{2,1,0:T(8,128)(2,1)S(1)}, bf16[8,256,256]{2,1,0:T(8,128)(2,1)S(1)}) fusion(f32[8,256,256]{2,1,0:T(8,128)} %reshape.112, bf16[8,512,256]{2,1,0:T(8,128)(2,1)} %bitcast.76, f32[8,256,256]{2,1,0:T(8,128)} %reshape.113), kind=kLoop, calls=%fused_computation.9 | loop fusion | flops 3145728 | bytes 8388608 | tf_op jit(solution)/shard_map/convert_element_type | solution.py:70
  189.2 1.5 convolution_convert_fusion.3
  190.6 3.6 %all-to-all-start.3 = ((bf16[8,32,2048]{2,1,0:T(8,128)(2,1)}), bf16[8,32,2048]{2,1,0:T(8,128)(2,1)S(1)}, u32[]{:S(2)}, u32[]{:S(2)}) async-start(bf16[8,32,2048]{2,1,0:T(8,128)(2,1)} %bitcast.15), calls=%async_computation.3 | async-start | bytes 2097152 | tf_op jit(solution)/shard_map/all_to_all | solution.py:76
  194.2 0.0 copy-start.2
  194.2 1.4 convolution_convert_fusion.1
  195.7 14.8 %all-to-all-done.3 = bf16[8,32,2048]{2,1,0:T(8,128)(2,1)S(1)} async-done(((bf16[8,32,2048]{2,1,0:T(8,128)(2,1)}), bf16[8,32,2048]{2,1,0:T(8,128)(2,1)S(1)}, u32[]{:S(2)}, u32[]{:S(2)}) %all-to-all-start.3) | async-done | bytes 1048608 | tf_op jit(solution)/shard_map/all_to_all | solution.py:76
  210.5 3.6 %all-to-all-start.6 = ((bf16[8,32,2048]{2,1,0:T(8,128)(2,1)}), bf16[8,32,2048]{2,1,0:T(8,128)(2,1)S(1)}, u32[]{:S(2)}, u32[]{:S(2)}) async-start(bf16[8,32,2048]{2,1,0:T(8,128)(2,1)} %bitcast.29), calls=%async_computation.6 | async-start | bytes 2097152 | tf_op jit(solution)/shard_map/all_to_all | solution.py:76
  214.1 0.0 copy-done.2
  214.1 0.1 copy.25
  214.2 0.2 broadcast_select_fusion.1
  214.4 0.2 select_n.39
  214.6 0.5 convolution_convert_fusion.2
  215.1 15.7 %all-to-all-done.6 = bf16[8,32,2048]{2,1,0:T(8,128)(2,1)S(1)} async-done(((bf16[8,32,2048]{2,1,0:T(8,128)(2,1)}), bf16[8,32,2048]{2,1,0:T(8,128)(2,1)S(1)}, u32[]{:S(2)}, u32[]{:S(2)}) %all-to-all-start.6) | async-done | bytes 1048608 | tf_op jit(solution)/shard_map/all_to_all | solution.py:76
  230.8 0.5 convolution_convert_fusion
  231.3 1.5 pad_maximum_fusion
  (7 shorter events, 0.1 us)
Async XLA Ops:
  0.0 8.1 %copy-start.3 = (f32[8,512]{1,0:T(8,128)S(1)}, f32[8,512]{1,0:T(8,128)}, u32[]{:S(2)}) copy-start(f32[8,512]{1,0:T(8,128)} %param.8) | copy-start | bytes 49156
  0.9 22.9 %copy-start = (bf16[4096,256]{1,0:T(8,128)(2,1)S(1)}, bf16[4096,256]{1,0:T(8,128)(2,1)}, u32[]{:S(2)}) copy-start(bf16[4096,256]{1,0:T(8,128)(2,1)} %param.6) | copy-start | bytes 6291460
  2.0 21.8 %all-to-all-start = ((bf16[8,128,512]{2,1,0:T(8,128)(2,1)}), bf16[8,128,512]{2,1,0:T(8,128)(2,1)S(1)}, u32[]{:S(2)}, u32[]{:S(2)}) async-start(bf16[8,128,512]{2,1,0:T(8,128)(2,1)} %stack.2), calls=%async_computation | async-start | bytes 2097152 | tf_op jit(solution)/shard_map/all_to_all | solution.py:37
  26.1 43.9 %all-to-all-start.4 = ((bf16[256,8,256]{2,1,0:T(8,128)(2,1)}), bf16[256,8,256]{2,1,0:T(8,128)(2,1)}, u32[]{:S(2)}, u32[]{:S(2)}) async-start(bf16[256,8,256]{2,1,0:T(8,128)(2,1)} %copy.27), calls=%async_computation.4 | async-start | bytes 2097152 | tf_op jit(solution)/shard_map/all_to_all | solution.py:63
  70.0 37.7 %all-to-all-start.1 = ((bf16[256,8,256]{2,1,0:T(8,128)(2,1)}), bf16[256,8,256]{2,1,0:T(8,128)(2,1)S(1)}, u32[]{:S(2)}, u32[]{:S(2)}) async-start(bf16[256,8,256]{2,1,0:T(8,128)(2,1)} %copy.21), calls=%async_computation.1 | async-start | bytes 2097152 | tf_op jit(solution)/shard_map/all_to_all | solution.py:63
  107.7 37.8 %all-to-all-start.5 = ((bf16[512,4,256]{2,1,0:T(4,128)(2,1)}), bf16[512,4,256]{2,1,0:T(4,128)(2,1)S(1)}, u32[]{:S(2)}, u32[]{:S(2)}) async-start(bf16[512,4,256]{2,1,0:T(4,128)(2,1)} %copy.29), calls=%async_computation.5 | async-start | bytes 2097152 | tf_op jit(solution)/shard_map/all_to_all | solution.py:67
  117.9 37.1 %copy-start.1 = (bf16[8,32,32]{2,1,0:T(8,128)(2,1)S(1)}, bf16[8,32,32]{2,1,0:T(8,128)(2,1)}, u32[]{:S(2)}) copy-start(bf16[8,32,32]{2,1,0:T(8,128)(2,1)} %param.10) | copy-start | bytes 49156
  145.5 37.9 %all-to-all-start.2 = ((bf16[512,4,256]{2,1,0:T(4,128)(2,1)}), bf16[512,4,256]{2,1,0:T(4,128)(2,1)S(1)}, u32[]{:S(2)}, u32[]{:S(2)}) async-start(bf16[512,4,256]{2,1,0:T(4,128)(2,1)} %copy.23), calls=%async_computation.2 | async-start | bytes 2097152 | tf_op jit(solution)/shard_map/all_to_all | solution.py:67
  190.6 19.9 %all-to-all-start.3 = ((bf16[8,32,2048]{2,1,0:T(8,128)(2,1)}), bf16[8,32,2048]{2,1,0:T(8,128)(2,1)S(1)}, u32[]{:S(2)}, u32[]{:S(2)}) async-start(bf16[8,32,2048]{2,1,0:T(8,128)(2,1)} %bitcast.15), calls=%async_computation.3 | async-start | bytes 2097152 | tf_op jit(solution)/shard_map/all_to_all | solution.py:76
  194.2 19.9 %copy-start.2 = (bf16[4,64,64]{2,1,0:T(8,128)(2,1)S(1)}, bf16[4,64,64]{2,1,0:T(8,128)(2,1)}, u32[]{:S(2)}) copy-start(bf16[4,64,64]{2,1,0:T(8,128)(2,1)} %param.11) | copy-start | bytes 98308
  210.5 20.3 %all-to-all-start.6 = ((bf16[8,32,2048]{2,1,0:T(8,128)(2,1)}), bf16[8,32,2048]{2,1,0:T(8,128)(2,1)S(1)}, u32[]{:S(2)}, u32[]{:S(2)}) async-start(bf16[8,32,2048]{2,1,0:T(8,128)(2,1)} %bitcast.29), calls=%async_computation.6 | async-start | bytes 2097152 | tf_op jit(solution)/shard_map/all_to_all | solution.py:76
